TPU v7x, 128 devices: a whole 4x4x4 slice. The times are simulated.
128 devices in a mesh: ctl: 32 (over y, z_lo, x), side: 2 (over core), tp: 2 (over z_hi).
Axes of the slice: x: 4, y: 4, z: 4 (z_hi: 2, z_lo: 2; z = z_hi * 2 + z_lo), core: 2. Of those that a mesh axis runs over, the one named last changes fastest.
Arguments:
- image_latent: bfloat16 [64, 256, 3072], P('ctl'), may hold values from -6 to 6
- control_latent: bfloat16 [64, 256, 3072], P('ctl'), may hold values from -6 to 6
- control_order: int32 [64, 256], P('ctl'), may hold values from 0 to 255, each once within a row
- captions: bfloat16 [128, 128, 3072], P('ctl'), may hold values from -6 to 6
- caption_ids: int32 [64], P('ctl'), may hold values from 0 to 3
- modulation: float32 [2, 64, 3, 3072], P('side', 'ctl'), may hold values from -3 to 3
- qkv_weight: bfloat16 [2, 3072, 3, 1536], P('side', 'ctl', None, 'tp'), may hold values from -1 to 1
- qk_gain: float32 [2, 2, 128], P('side'), may hold values from 1 to 6
- out_weight: bfloat16 [2, 1536, 3072], P('side', 'tp', 'ctl'), may hold values from -0.5 to 0.5
- zero_weight: bfloat16 [3072, 3072], P('ctl', 'tp'), may hold values from -0.109375 to 0.109375
- proj_weight: bfloat16 [3072, 64], P('tp'), may hold values from -1 to 1
- final_mod: float32 [64, 2, 3072], P('ctl'), may hold values from -3 to 3
- velocity_target: float32 [64, 256, 64], P('ctl'), may hold values from -6 to 6
Outputs:
- hidden_out: bfloat16 [2, 64, 256, 3072], P('side', 'ctl', None, 'tp')
- zero_grad: float32 [3072, 3072], P(('ctl', 'side'), 'tp')
Inputs may be any that keep to these rules, and one draw needn't show every extreme that they name: caption_ids counts from the first caption held by the sample's own index of ctl. Each sample's row of control_order is a permutation.
All inputs are finite; a program needn't handle non-finite values.
Results may differ from a plain program's by a relative error of at most 0.03.
Values may be sent and summed in bfloat16 or wider, within the bound.
No kernel may reach another device: no remote copies, remote signals or barrier semaphores. Data moves between devices by JAX's collectives and lax.ppermute only.
A program may use at most 192 MiB of HBM per device.

v0:
```python
import math
import jax
import jax.numpy as jnp
from jax import lax
from jax.sharding import PartitionSpec as P

HEAD_DIM = 128
EPS = 1e-06


def passed_along(shard, axis, by):
    length = lax.axis_size(axis)
    pairs = [(i, i + by) for i in range(length) if 0 <= i + by < length]
    return lax.ppermute(shard, axis, pairs)


def partner(value, axis, bit):
    mask = 2**bit
    pairs = [(source, source ^ mask) for source in range(lax.axis_size(axis))]
    return lax.ppermute(value, axis, pairs)


def layer_norm(values):
    center = values - jnp.mean(values, axis=-1, keepdims=True)
    spread = jnp.mean(center * center, axis=-1, keepdims=True)
    return center * lax.rsqrt(spread + EPS)


def head_norm(values, gain_row):
    power_mean = jnp.mean(values * values, axis=-1, keepdims=True)
    return (values * lax.rsqrt(power_mean + EPS) * gain_row).astype(jnp.bfloat16)


def rounded(values):
    narrow = lax.optimization_barrier(values.astype(jnp.bfloat16))
    return narrow.astype(jnp.float32)


def local(
    image_latent,
    control_latent,
    control_order,
    captions,
    caption_ids,
    modulation,
    qkv_weight,
    qk_gain,
    out_weight,
    zero_weight,
    proj_weight,
    final_mod,
    velocity_target,
):
    side_index = lax.axis_index("side")
    tp_index = lax.axis_index("tp")
    ctl_count = lax.axis_size("ctl")
    tp_count = lax.axis_size("tp")
    is_control = side_index == 0
    micro_count, img_rows, width_full = image_latent.shape
    text_rows = captions.shape[1]
    seq_rows = text_rows + img_rows
    local_heads = qkv_weight.shape[3]
    head_count = local_heads // HEAD_DIM
    half_width = width_full // tp_count
    quarter_width = half_width // 2
    flat_rows = micro_count * img_rows
    block_rows = width_full // (2 * ctl_count)
    aligned = jax.vmap(lambda latent, order_row: jnp.take(latent, order_row, axis=0))(
        control_latent, control_order
    )
    plain_rows = image_latent.astype(jnp.float32)
    hidden = plain_rows + jnp.where(is_control, 1.0, 0.0) * aligned.astype(jnp.float32)
    chosen = jnp.take(captions, caption_ids, axis=0).astype(jnp.float32)
    sequence = jnp.concatenate([chosen, hidden], axis=1)
    modulate = modulation[0]
    normed = (layer_norm(sequence) * (1.0 + modulate[:, 1:2]) + modulate[:, 0:1]).astype(
        jnp.bfloat16
    )
    text_flat = normed.reshape(micro_count * seq_rows, width_full)
    image_flat = normed[:, text_rows:].reshape(flat_rows, width_full)
    shard_piece = lax.all_gather(qkv_weight, "ctl", axis=1, tiled=True)
    count_rows = shard_piece.shape[1]
    query_acc = jnp.dot(image_flat, shard_piece[0, :, 0], preferred_element_type=jnp.float32)
    pair_weight = shard_piece[0, :, 1:].reshape(count_rows, 2 * local_heads)
    pair_acc = jnp.dot(text_flat, pair_weight, preferred_element_type=jnp.float32)
    query_acc, pair_acc = (query_acc, pair_acc)
    gain_pair = qk_gain[0]
    queries = head_norm(
        query_acc.reshape(micro_count, img_rows, head_count, HEAD_DIM), gain_pair[0]
    )
    pair_acc = pair_acc.reshape(micro_count, seq_rows, 2, head_count, HEAD_DIM)
    keys_all = head_norm(pair_acc[:, :, 0], gain_pair[1])
    values_all = pair_acc[:, :, 1].astype(jnp.bfloat16)
    scores = jnp.einsum(
        "bihd,bjhd->bhij", queries, keys_all, preferred_element_type=jnp.float32
    ) / math.sqrt(HEAD_DIM)
    attend = jax.nn.softmax(scores, axis=-1).astype(jnp.bfloat16)
    mixed_heads = jnp.einsum(
        "bhij,bjhd->bihd", attend, values_all, preferred_element_type=jnp.float32
    )
    mixed_heads = mixed_heads.astype(jnp.bfloat16).reshape(flat_rows, local_heads)
    partial_value = rounded(
        jnp.dot(
            mixed_heads,
            lax.all_gather(out_weight, "ctl", axis=2, tiled=True)[0],
            preferred_element_type=jnp.float32,
        )
    )
    head_sum = lax.psum_scatter(
        partial_value.astype(jnp.bfloat16), "tp", scatter_dimension=1, tiled=True
    ).astype(jnp.float32)
    hid_half = lax.dynamic_slice_in_dim(hidden, tp_index * half_width, half_width, 2)
    gate_half = lax.dynamic_slice_in_dim(modulate[:, 2:3], tp_index * half_width, half_width, 2)
    act_half = hid_half + gate_half * head_sum.reshape(micro_count, img_rows, half_width)
    act_half = act_half.reshape(flat_rows, half_width)
    act_narrow = lax.all_gather(act_half.astype(jnp.bfloat16), "tp", axis=1, tiled=True)
    act_other = passed_along(act_narrow, "side", 1)
    control_rows = jnp.where(is_control, act_narrow, act_other)
    own_cols = lax.dynamic_slice_in_dim(zero_weight, side_index * quarter_width, quarter_width, 1)
    columns = control_rows
    own_part = jnp.dot(
        columns,
        lax.all_gather(own_cols, "ctl", axis=0, tiled=True),
        preferred_element_type=jnp.float32,
    )
    own_narrow = own_part.astype(jnp.bfloat16)
    other_narrow = partner(own_narrow, "side", 0)
    residual_narrow = jnp.where(
        is_control,
        jnp.concatenate([own_narrow, other_narrow], axis=1),
        jnp.concatenate([other_narrow, own_narrow], axis=1),
    )
    merged = act_half + residual_narrow.astype(jnp.float32)
    section_out = jnp.where(is_control, residual_narrow, merged.astype(jnp.bfloat16))
    final_half = lax.dynamic_slice_in_dim(final_mod, tp_index * half_width, half_width, 2)
    merged_rows = merged.reshape(micro_count, img_rows, half_width)
    row_total, squares = lax.psum(
        (
            jnp.sum(merged_rows, axis=-1, keepdims=True),
            jnp.sum(merged_rows * merged_rows, axis=-1, keepdims=True),
        ),
        "tp",
    )
    mean_val = row_total / width_full
    spread = squares / width_full - mean_val * mean_val
    scale_inv = lax.rsqrt(spread + EPS)
    unit_rows = (merged_rows - mean_val) * scale_inv
    final_in = (unit_rows * (1.0 + final_half[:, 1:2]) + final_half[:, 0:1]).astype(jnp.bfloat16)
    prediction = lax.psum(
        jnp.dot(
            final_in.reshape(flat_rows, half_width), proj_weight, preferred_element_type=jnp.float32
        ).astype(jnp.bfloat16),
        "tp",
    ).astype(jnp.float32)
    loss_factor = 4.0 / math.sqrt(micro_count * ctl_count * img_rows)
    grad_pred = (loss_factor * (prediction - velocity_target.reshape(flat_rows, -1))).astype(
        jnp.bfloat16
    )
    grad_unit = lax.dot_general(
        grad_pred, proj_weight, (((1,), (1,)), ((), ())), preferred_element_type=jnp.float32
    )
    grad_unit = grad_unit.reshape(micro_count, img_rows, half_width) * (1.0 + final_half[:, 1:2])
    first_sum, second_sum = lax.psum(
        (
            jnp.sum(grad_unit, axis=-1, keepdims=True),
            jnp.sum(grad_unit * unit_rows, axis=-1, keepdims=True),
        ),
        "tp",
    )
    grad_narrow = (
        (grad_unit - first_sum / width_full - unit_rows * (second_sum / width_full)) * scale_inv
    ).astype(jnp.bfloat16)
    grad_narrow = grad_narrow.reshape(flat_rows, half_width)
    returned = passed_along(grad_narrow, "side", -1)
    grad_rows_all = jnp.where(is_control, returned, grad_narrow)
    own_act = lax.dynamic_index_in_dim(
        control_rows.reshape(flat_rows, ctl_count, 2, block_rows), side_index, 2, keepdims=False
    )
    own_act = own_act.reshape(flat_rows, ctl_count * block_rows)
    columns = own_act
    product = lax.dot_general(
        columns, grad_rows_all, (((0,), (0,)), ((), ())), preferred_element_type=jnp.float32
    )
    zero_grad = lax.psum_scatter(
        rounded(product).astype(jnp.bfloat16), "ctl", scatter_dimension=0, tiled=True
    ).astype(jnp.float32)
    return (section_out.reshape(1, micro_count, img_rows, half_width), zero_grad)


def solution(mesh):
    return jax.shard_map(
        local,
        mesh=mesh,
        in_specs=(
            P("ctl", None, None),
            P("ctl", None, None),
            P("ctl", None),
            P("ctl", None, None),
            P("ctl"),
            P("side", "ctl", None, None),
            P("side", "ctl", None, "tp"),
            P("side", None, None),
            P("side", "tp", "ctl"),
            P("ctl", "tp"),
            P("tp", None),
            P("ctl", None, None),
            P("ctl", None, None),
        ),
        out_specs=(P("side", "ctl", None, "tp"), P(("ctl", "side"), "tp")),
        check_vma=False,
    )
```

profile of v0, /device:TPU:0, one launch (start us, length us, event | category | flops | bytes accessed | tf_op | source)
XLA Modules:
  0.0 868.4 jit_solution(13904714863020489514)
XLA Ops:
  12.2 14.7 %gather_fusion.1 = bf16[512,3072]{1,0:T(8,128)(2,1)} fusion(bf16[2,256,3072]{2,1,0:T(8,128)(2,1)S(1)} %copy-done, s32[512]{0:T(512)S(1)} %bitcast.114), kind=kCustom, calls=%fused_computation.1 | custom fusion | bytes 6295552 | tf_op jit(solution)/shard_map/vmap(jit(_take))/gather | solution.py:68
  26.9 7.2 multiply_add_fusion
  37.8 3.5 fusion.1
  42.7 3.7 add_convert_fusion
  46.4 144.6 %all-gather.5.cloned.1.call-done = bf16[1,3072,3,768]{3,1,2,0:T(8,128)(2,1)} async-done(((bf16[1,96,3,768]{3,1,2,0:T(8,128)(2,1)}), bf16[1,3072,3,768]{3,1,2,0:T(8,128)(2,1)}) %all-gather.5.cloned.1.call-update) | async-done | bytes 14155792 | tf_op jit(solution)/shard_map/all_gather | solution.py:81
  191.0 7.8 slice.59
  198.9 12.7 %copy.37 = bf16[1,3072,2,768]{1,3,2,0:T(8,128)(2,1)} copy(bf16[1,3072,2,768]{3,1,2,0:T(8,128)(2,1)} %slice.59) | data formatting | bytes 18874368
  211.5 4.8 slice_bitcast_fusion
  216.3 6.7 copy.25
  223.0 11.8 %fusion.2 = f32[2,384,2,6,128]{1,4,3,2,0:T(8,128)S(1)} fusion(bf16[2,6,128,3072,1]{3,2,1,0,4:T(8,128)(2,1)} %bitcast.117, bf16[2,384,3072]{2,1,0:T(8,128)(2,1)} %add_convert_fusion), kind=kOutput, calls=%fused_computation.10 | convolution fusion | flops 7247757312 | bytes 18874368 | tf_op jit(solution)/shard_map/dot_general | solution.py:85
  235.1 6.0 multiply_reduce_fusion.5
  242.1 2.1 copy-done.3
  245.9 10.0 %fusion.21 = bf16[2,256,6,128]{1,3,2,0:T(8,128)(2,1)S(1)} fusion(f32[2,6,256]{2,1,0:T(8,128)S(1)} %fusion.44, f32[2,384,2,6,128]{1,4,3,2,0:T(8,128)} %copy-done.7, f32[2,6,256,384]{3,2,1,0:T(8,128)} %copy-done.3), kind=kOutput, calls=%fused_computation.48 | convolution fusion | flops 308284800 | bytes 11415552 | tf_op jit(solution)/shard_map/bhij,bjhd->bihd/dot_general | solution.py:98
  257.0 91.9 %all-gather.7.cloned.1.call-done = bf16[1,768,3072]{1,2,0:T(8,128)(2,1)} async-done(((bf16[1,768,96]{1,2,0:T(8,128)(2,1)}), bf16[1,768,3072]{1,2,0:T(8,128)(2,1)}) %all-gather.7.cloned.1.call-update) | async-done | bytes 4718608 | tf_op jit(solution)/shard_map/all_gather | solution.py:105
  348.9 6.4 fusion.6
  355.4 47.4 %reduce-scatter.3.cloned.1.call-done = bf16[512,1536]{1,0:T(8,128)(2,1)} async-done(((bf16[512,3072]{1,0:T(8,128)(2,1)}), bf16[512,1536]{1,0:T(8,128)(2,1)}) %reduce-scatter.3.cloned.1.call-update) | async-done | bytes 1572880 | tf_op jit(solution)/shard_map/reduce_scatter | solution.py:109
  402.8 2.8 fusion.17
  408.3 47.6 %all-gather.9.cloned.1.call-done = bf16[512,3072]{0,1:T(8,128)(2,1)} async-done(((bf16[512,1536]{0,1:T(8,128)(2,1)}), bf16[512,3072]{0,1:T(8,128)(2,1)}) %all-gather.9.cloned.1.call-update) | async-done | bytes 3145744 | tf_op jit(solution)/shard_map/all_gather | solution.py:116
  457.7 5.3 collective-permute-done
  463.0 2.3 broadcast_select_fusion
  465.3 149.6 %all-gather.11.cloned.1.call-done = bf16[3072,768]{1,0:T(8,128)(2,1)} async-done(((bf16[96,768]{1,0:T(8,128)(2,1)}), bf16[3072,768]{1,0:T(8,128)(2,1)}) %all-gather.11.cloned.1.call-update) | async-done | bytes 4718608 | tf_op jit(solution)/shard_map/all_gather | solution.py:123
  614.9 5.9 convolution_convert_fusion.1
  620.9 2.5 collective-permute-done.1
  623.4 3.9 fusion.42
  627.3 6.6 all-reduce.1
  636.8 28.0 %all-reduce.4.cloned.1.call-done = bf16[512,64]{0,1:T(8,128)(2,1)} async-done(((bf16[512,64]{0,1:T(8,128)(2,1)}), bf16[512,64]{0,1:T(8,128)(2,1)}) %all-reduce.4.cloned.1.call-update) | async-done | bytes 65552 | tf_op jit(solution)/shard_map/psum | solution.py:149
  668.0 6.4 all-reduce
  674.4 4.0 multiply_convert_fusion
  681.2 2.7 collective-permute-done.2
  683.9 4.2 convolution_convert_fusion
  688.2 4.7 select_bitcast_fusion
  692.8 167.0 %reduce-scatter.5.cloned.1.call-done = bf16[48,1536]{1,0:T(8,128)(2,1)} async-done(((bf16[1536,1536]{1,0:T(8,128)(2,1)}), bf16[48,1536]{1,0:T(8,128)(2,1)}) %reduce-scatter.5.cloned.1.call-update) | async-done | bytes 147472 | tf_op jit(solution)/shard_map/reduce_scatter | solution.py:184
  (83 shorter events, 29.0 us)
Async XLA Ops:
  7.2 5.0 copy-start
  7.2 183.8 %all-gather.5.cloned.1.call-start = ((), (), s32[]{:S(2)}) async-start(), calls=%async_computation.2 | async-start | bytes 14598144 | tf_op jit(solution)/shard_map/all_gather | solution.py:81
  7.9 340.9 %all-gather.7.cloned.1.call-start = ((), (), s32[]{:S(2)}) async-start(), calls=%async_computation.3 | async-start | bytes 4866048 | tf_op jit(solution)/shard_map/all_gather | solution.py:105
  8.7 394.1 %reduce-scatter.3.cloned.1.call-start = ((), (), s32[]{:S(2)}) async-start(), calls=%async_computation.4 | async-start | bytes 4718592 | tf_op jit(solution)/shard_map/reduce_scatter | solution.py:109
  26.9 7.2 copy-start.8
  35.9 5.4 slice-start
  37.8 3.7 slice-start.1
  41.4 1.3 copy-start.11
  223.0 12.1 %copy-start.6 = (bf16[768,3072]{1,0:T(8,128)(2,1)S(1)}, bf16[768,3072]{1,0:T(8,128)(2,1)}, u32[]{:S(2)}) copy-start(bf16[768,3072]{1,0:T(8,128)(2,1)} %copy.25) | copy-start | bytes 14155780
  234.9 6.3 copy-start.7
  242.1 2.1 copy-start.3
  355.3 100.6 %all-gather.9.cloned.1.call-start = ((), (), s32[]{:S(2)}) async-start(), calls=%async_computation.5 | async-start | bytes 4718592 | tf_op jit(solution)/shard_map/all_gather | solution.py:116
  405.6 1.9 copy-start.10
  407.5 207.4 %all-gather.11.cloned.1.call-start = ((), (), s32[]{:S(2)}) async-start(), calls=%async_computation.6 | async-start | bytes 4866048 | tf_op jit(solution)/shard_map/all_gather | solution.py:123
  408.2 256.6 %all-reduce.4.cloned.1.call-start = ((), (), s32[]{:S(2)}) async-start(), calls=%async_computation.7 | async-start | bytes 131072 | tf_op jit(solution)/shard_map/psum | solution.py:149
  455.9 7.0 collective-permute-start
  465.3 155.5 %copy-start.5 = (bf16[512,3072]{0,1:T(8,128)(2,1)}, bf16[512,3072]{0,1:T(8,128)(2,1)S(1)}, u32[]{:S(2)}) copy-start(bf16[512,3072]{0,1:T(8,128)(2,1)S(1)} %broadcast_select_fusion) | copy-start | bytes 9437188
  465.3 155.5 %copy-start.12 = (f32[2,2,3072]{2,1,0:T(2,128)S(1)}, f32[2,2,3072]{2,1,0:T(2,128)}, u32[]{:S(2)}) copy-start(f32[2,2,3072]{2,1,0:T(2,128)} %param.24) | copy-start | bytes 147460
  620.8 2.6 collective-permute-start.1
  627.3 47.1 %copy-start.2 = (f32[2,256,1536]{2,1,0:T(8,128)}, f32[2,256,1536]{2,1,0:T(8,128)S(1)}, u32[]{:S(2)}) copy-start(f32[2,256,1536]{2,1,0:T(8,128)S(1)} %get-tuple-element.8) | copy-start | bytes 9437188
  627.3 7.2 copy-start.9
  635.8 224.0 %reduce-scatter.5.cloned.1.call-start = ((), (), s32[]{:S(2)}) async-start(), calls=%async_computation.8 | async-start | bytes 4866048 | tf_op jit(solution)/shard_map/reduce_scatter | solution.py:184
  666.3 1.7 copy-start.4
  678.4 5.5 collective-permute-start.2
  688.1 173.4 %copy-start.1 = (bf16[2,256,3072]{2,1,0:T(8,128)(2,1)S(1)}, bf16[2,256,3072]{2,1,0:T(8,128)(2,1)}, u32[]{:S(2)}) copy-start(bf16[2,256,3072]{2,1,0:T(8,128)(2,1)} %param.14) | copy-start | bytes 9437188
Sparse Core Ops, SparseCore 0:
  9.6 181.3 all-gather.4
  192.7 156.1 all-gather.6
  355.4 47.3 reduce-scatter.2
  407.6 48.2 all-gather.8
  458.0 156.8 all-gather.10
  635.9 28.8 all-reduce.3
  688.3 171.5 reduce-scatter.4
where the time goes:
time: 869 us; the launch traced here: 868 us
  waiting for transfers between devices  688 us (79%)
  local copies, waits for them, and re-layouts  58.5 us (7%)
  matrix products  48.1 us (6%)
  other arithmetic  42.8 us (5%)
  between operations  14.5 us (2%)
  blocking collectives  13 us (1%)
    reduce_scatter x1, waiting for transfers between devices, local(): lax.psum_scatter(rounded(product).astype(jnp.bfloat16), 'ctl', scatter_di...  167 us
    all_gather x1, waiting for transfers between devices, local(): lax.all_gather(own_cols, 'ctl', axis=0, tiled=True)  150 us
    all_gather x1, waiting for transfers between devices, local(): shard_piece = lax.all_gather(qkv_weight, 'ctl', axis=1, tiled=True)  145 us
    all_gather x1, waiting for transfers between devices, local(): lax.all_gather(out_weight, 'ctl', axis=2, tiled=True)[0]  91.9 us
    all_gather x1, waiting for transfers between devices, local(): lax.all_gather(act_half.astype(jnp.bfloat16), 'tp', axis=1, tiled=True)  47.6 us
    reduce_scatter x1, waiting for transfers between devices, local(): lax.psum_scatter(partial_value.astype(jnp.bfloat16), 'tp', scatter_dimens...  47.4 us
    psum x1, waiting for transfers between devices, local(): lax.psum(jnp.dot(final_in.reshape(flat_rows, half_width), proj_weight, pr...  28 us
  transfers between devices with their start and end apart: 10, of which 10 were waited for; matrix products, arithmetic and copies ran while one was open for 13% of the time, Pallas kernels for 0%

commit v1 on v0

--- a/solution.py
+++ b/solution.py
@@ -120,7 +120,9 @@
     columns = control_rows
     own_part = jnp.dot(
         columns,
-        lax.all_gather(own_cols, "ctl", axis=0, tiled=True),
+        jnp.concatenate(
+            lax.all_to_all(jnp.stack([own_cols] * lax.axis_size("ctl")), "ctl", 0, 0), axis=0
+        ),
         preferred_element_type=jnp.float32,
     )
     own_narrow = own_part.astype(jnp.bfloat16)

time: 869 us -> 771 us (0.89)
  waiting for transfers between devices: 688 us -> 579 us
    all_gather x1 -> x0, waiting for transfers between devices: 150 us -> none  [local(): lax.all_gather(own_cols, 'ctl', axis=0, tiled=True)]
    all_gather x1, waiting for transfers between devices: 47.6 us -> 86.6 us  [local(): lax.all_gather(act_half.astype(jnp.bfloat16), 'tp', axis=1, tiled=True)]
  transfers between devices with their start and end apart: 10 -> 10, of which waited for: 10 -> 9; matrix products, arithmetic and copies ran while one was open for 13% -> 15% of each run, Pallas kernels for 0% -> 0%
where the time goes in v1:
time: 771 us; the launch traced here: 770 us
  waiting for transfers between devices  579 us (75%)
  local copies, waits for them, and re-layouts  60.6 us (8%)
  matrix products  49.3 us (6%)
  other arithmetic  42.9 us (6%)
  between operations  14.5 us (2%)
  blocking collectives  13 us (2%)
  starting transfers between devices  10.9 us (1%)
    reduce_scatter x1, waiting for transfers between devices, local(): lax.psum_scatter(rounded(product).astype(jnp.bfloat16), 'ctl', scatter_di...  167 us
    all_gather x1, waiting for transfers between devices, local(): shard_piece = lax.all_gather(qkv_weight, 'ctl', axis=1, tiled=True)  145 us
    all_gather x1, waiting for transfers between devices, local(): lax.all_gather(out_weight, 'ctl', axis=2, tiled=True)[0]  91.6 us
    all_gather x1, waiting for transfers between devices, local(): lax.all_gather(act_half.astype(jnp.bfloat16), 'tp', axis=1, tiled=True)  86.6 us
    reduce_scatter x1, waiting for transfers between devices, local(): lax.psum_scatter(partial_value.astype(jnp.bfloat16), 'tp', scatter_dimens...  47.8 us
    psum x1, waiting for transfers between devices, local(): lax.psum(jnp.dot(final_in.reshape(flat_rows, half_width), proj_weight, pr...  28.6 us
    unnamed x34, local copies, waits for them, and re-layouts  16.2 us
  transfers between devices with their start and end apart: 10, of which 9 were waited for; matrix products, arithmetic and copies ran while one was open for 15% of the time, Pallas kernels for 0%

profile of v1, /device:TPU:0, one launch (start us, length us, event | category | flops | bytes accessed | tf_op | source)
XLA Modules:
  0.0 769.7 jit_solution(9345542139527392135)
XLA Ops:
  12.2 14.8 %gather_fusion.1 = bf16[512,3072]{1,0:T(8,128)(2,1)} fusion(bf16[2,256,3072]{2,1,0:T(8,128)(2,1)S(1)} %copy-done, s32[512]{0:T(512)S(1)} %bitcast.115), kind=kCustom, calls=%fused_computation.1 | custom fusion | bytes 6295552 | tf_op jit(solution)/shard_map/vmap(jit(_take))/gather | solution.py:68
  26.9 7.2 multiply_add_fusion
  37.8 3.5 fusion.1
  42.7 3.7 add_convert_fusion
  46.4 145.0 %all-gather.4.cloned.1.call-done = bf16[1,3072,3,768]{3,1,2,0:T(8,128)(2,1)} async-done(((bf16[1,96,3,768]{3,1,2,0:T(8,128)(2,1)}), bf16[1,3072,3,768]{3,1,2,0:T(8,128)(2,1)}) %all-gather.4.cloned.1.call-update) | async-done | bytes 14155792 | tf_op jit(solution)/shard_map/all_gather | solution.py:81
  191.5 7.9 %slice.59 = bf16[1,3072,2,768]{3,1,2,0:T(8,128)(2,1)} slice(bf16[1,3072,3,768]{3,1,2,0:T(8,128)(2,1)} %all-gather.4.cloned.1.call-done), slice={[0:1], [0:3072], [1:3], [0:768]} | slice | bytes 18874368 | tf_op jit(solution)/shard_map/slice | solution.py:84
  199.3 12.7 %copy.37 = bf16[1,3072,2,768]{1,3,2,0:T(8,128)(2,1)} copy(bf16[1,3072,2,768]{3,1,2,0:T(8,128)(2,1)} %slice.59) | data formatting | bytes 18874368
  212.0 4.8 slice_bitcast_fusion
  216.8 6.7 copy.25
  223.5 11.8 %fusion.2 = f32[2,384,2,6,128]{1,4,3,2,0:T(8,128)S(1)} fusion(bf16[2,6,128,3072,1]{3,2,1,0,4:T(8,128)(2,1)} %bitcast.118, bf16[2,384,3072]{2,1,0:T(8,128)(2,1)} %add_convert_fusion), kind=kOutput, calls=%fused_computation.10 | convolution fusion | flops 7247757312 | bytes 18874368 | tf_op jit(solution)/shard_map/dot_general | solution.py:85
  235.5 6.0 multiply_reduce_fusion.5
  246.4 10.0 %fusion.21 = bf16[2,256,6,128]{1,3,2,0:T(8,128)(2,1)S(1)} fusion(f32[2,6,256]{2,1,0:T(8,128)S(1)} %fusion.44, f32[2,384,2,6,128]{1,4,3,2,0:T(8,128)} %copy-done.7, f32[2,6,256,384]{3,2,1,0:T(8,128)} %copy-done.3), kind=kOutput, calls=%fused_computation.48 | convolution fusion | flops 308284800 | bytes 11415552 | tf_op jit(solution)/shard_map/bhij,bjhd->bihd/dot_general | solution.py:98
  257.4 91.6 %all-gather.6.cloned.1.call-done = bf16[1,768,3072]{1,2,0:T(8,128)(2,1)} async-done(((bf16[1,768,96]{1,2,0:T(8,128)(2,1)}), bf16[1,768,3072]{1,2,0:T(8,128)(2,1)}) %all-gather.6.cloned.1.call-update) | async-done | bytes 4718608 | tf_op jit(solution)/shard_map/all_gather | solution.py:105
  349.0 6.4 fusion.6
  355.5 47.8 %reduce-scatter.3.cloned.1.call-done = bf16[512,1536]{1,0:T(8,128)(2,1)} async-done(((bf16[512,3072]{1,0:T(8,128)(2,1)}), bf16[512,1536]{1,0:T(8,128)(2,1)}) %reduce-scatter.3.cloned.1.call-update) | async-done | bytes 1572880 | tf_op jit(solution)/shard_map/reduce_scatter | solution.py:109
  403.3 2.8 fusion.17
  408.0 2.7 stack.2
  410.7 7.3 all-to-all-start
  418.0 86.6 %all-gather.8.cloned.1.call-done = bf16[512,3072]{0,1:T(8,128)(2,1)} async-done(((bf16[512,1536]{0,1:T(8,128)(2,1)}), bf16[512,3072]{0,1:T(8,128)(2,1)}) %all-gather.8.cloned.1.call-update) | async-done | bytes 3145744 | tf_op jit(solution)/shard_map/all_gather | solution.py:116
  506.7 5.3 collective-permute-done
  512.0 2.3 broadcast_select_fusion
  514.3 7.1 convolution_convert_fusion.1
  521.5 2.5 collective-permute-done.1
  524.0 4.0 fusion.42
  528.0 6.6 all-reduce.1
  537.5 28.6 %all-reduce.4.cloned.1.call-done = bf16[512,64]{0,1:T(8,128)(2,1)} async-done(((bf16[512,64]{0,1:T(8,128)(2,1)}), bf16[512,64]{0,1:T(8,128)(2,1)}) %all-reduce.4.cloned.1.call-update) | async-done | bytes 65552 | tf_op jit(solution)/shard_map/psum | solution.py:151
  569.3 6.4 all-reduce
  575.7 4.0 multiply_convert_fusion
  582.5 2.7 collective-permute-done.2
  585.2 4.2 convolution_convert_fusion
  589.4 4.7 select_bitcast_fusion
  594.1 167.1 %reduce-scatter.5.cloned.1.call-done = bf16[48,1536]{1,0:T(8,128)(2,1)} async-done(((bf16[1536,1536]{1,0:T(8,128)(2,1)}), bf16[48,1536]{1,0:T(8,128)(2,1)}) %reduce-scatter.5.cloned.1.call-update) | async-done | bytes 147472 | tf_op jit(solution)/shard_map/reduce_scatter | solution.py:186
  (83 shorter events, 30.8 us)
Async XLA Ops:
  7.2 5.0 copy-start
  7.2 184.3 %all-gather.4.cloned.1.call-start = ((), (), s32[]{:S(2)}) async-start(), calls=%async_computation.3 | async-start | bytes 14598144 | tf_op jit(solution)/shard_map/all_gather | solution.py:81
  7.9 341.0 %all-gather.6.cloned.1.call-start = ((), (), s32[]{:S(2)}) async-start(), calls=%async_computation.4 | async-start | bytes 4866048 | tf_op jit(solution)/shard_map/all_gather | solution.py:105
  8.7 394.6 %reduce-scatter.3.cloned.1.call-start = ((), (), s32[]{:S(2)}) async-start(), calls=%async_computation.5 | async-start | bytes 4718592 | tf_op jit(solution)/shard_map/reduce_scatter | solution.py:109
  26.9 7.2 copy-start.8
  35.9 5.4 slice-start
  37.8 3.7 slice-start.1
  41.4 1.3 copy-start.11
  223.5 12.1 %copy-start.6 = (bf16[768,3072]{1,0:T(8,128)(2,1)S(1)}, bf16[768,3072]{1,0:T(8,128)(2,1)}, u32[]{:S(2)}) copy-start(bf16[768,3072]{1,0:T(8,128)(2,1)} %copy.25) | copy-start | bytes 14155780
  235.3 6.3 copy-start.7
  242.5 2.1 copy-start.3
  355.4 149.2 %all-gather.8.cloned.1.call-start = ((), (), s32[]{:S(2)}) async-start(), calls=%async_computation.6 | async-start | bytes 4718592 | tf_op jit(solution)/shard_map/all_gather | solution.py:116
  406.1 1.8 copy-start.10
  410.7 103.6 %all-to-all-start = ((bf16[32,96,768]{2,1,0:T(8,128)(2,1)}), bf16[32,96,768]{2,1,0:T(8,128)(2,1)}, u32[]{:S(2)}, u32[]{:S(2)}) async-start(bf16[32,96,768]{2,1,0:T(8,128)(2,1)} %stack.2), calls=%async_computation.1 | async-start | bytes 9437184 | tf_op jit(solution)/shard_map/all_to_all | solution.py:124
  418.0 148.1 %all-reduce.4.cloned.1.call-start = ((), (), s32[]{:S(2)}) async-start(), calls=%async_computation.7 | async-start | bytes 131072 | tf_op jit(solution)/shard_map/psum | solution.py:151
  504.6 7.4 collective-permute-start
  514.3 7.1 copy-start.5
  514.3 7.1 copy-start.12
  521.4 2.6 collective-permute-start.1
  528.0 47.7 %copy-start.2 = (f32[2,256,1536]{2,1,0:T(8,128)}, f32[2,256,1536]{2,1,0:T(8,128)S(1)}, u32[]{:S(2)}) copy-start(f32[2,256,1536]{2,1,0:T(8,128)S(1)} %get-tuple-element.8) | copy-start | bytes 9437188
  528.0 7.2 copy-start.9
  536.5 224.7 %reduce-scatter.5.cloned.1.call-start = ((), (), s32[]{:S(2)}) async-start(), calls=%async_computation.8 | async-start | bytes 4866048 | tf_op jit(solution)/shard_map/reduce_scatter | solution.py:186
  567.6 1.7 copy-start.4
  579.7 5.5 collective-permute-start.2
  589.4 173.4 %copy-start.1 = (bf16[2,256,3072]{2,1,0:T(8,128)(2,1)S(1)}, bf16[2,256,3072]{2,1,0:T(8,128)(2,1)}, u32[]{:S(2)}) copy-start(bf16[2,256,3072]{2,1,0:T(8,128)(2,1)} %param.14) | copy-start | bytes 9437188
Sparse Core Ops, SparseCore 0:
  9.6 181.7 all-gather.3
  193.1 155.8 all-gather.5
  355.5 47.7 reduce-scatter.2
  408.1 96.4 all-gather.7
  536.6 29.4 all-reduce.3
  589.5 171.6 reduce-scatter.4
